TPU v7x, 32 devices: a whole 2x2x4 slice. The times are simulated.
32 devices in a mesh: seq: 16 (over z, y, core), head: 2 (over x).
Axes of the slice: x: 2, y: 2, z: 4, core: 2. Of those that a mesh axis runs over, the one named last changes fastest.
Arguments:
- queries: bfloat16 [4096, 4096], P(('seq', 'head')), may hold values from -6 to 6
- keys: bfloat16 [4096, 4096], P(('seq', 'head')), may hold values from -6 to 6
- values: bfloat16 [4096, 4096], P(('seq', 'head')), may hold values from -75 to 75
- out_weight: bfloat16 [4096, 4096], P('seq', 'head'), may hold values from -0.09375 to 0.09375
- norm_gain: float32 [4096], P('head'), may hold values from 0.5 to 1.5
Outputs:
- projected: bfloat16 [4096, 4096], P('seq', 'head')
All inputs are finite; a program needn't handle non-finite values.
Results may differ from a plain program's by a relative error of at most 0.0058.
Values may be sent and summed in bfloat16 or wider, within the bound.
No kernel may reach another device: no remote copies, remote signals or barrier semaphores. Data moves between devices by JAX's collectives and lax.ppermute only.
A program may use at most 128 MiB of HBM per device.

v0:
```python
import jax
import jax.numpy as jnp
from jax import lax
from jax.sharding import PartitionSpec as P

HEAD_DIM = 128


def carried_in(part, axis, combine, identity):
    place = lax.axis_index(axis)
    gathered = lax.all_gather(part, axis)
    state = jnp.zeros_like(part) + jnp.asarray(identity, part.dtype)

    def one(hop, state):
        return combine(state, lax.dynamic_index_in_dim(gathered, hop, 0, False))

    return lax.fori_loop(0, place, one, state)


def add_states(earlier, later):
    return earlier + later


def local(queries, keys, values, out_weight, norm_gain):
    heads_dev = norm_gain.shape[0] // HEAD_DIM
    query_block, key_block, value_block = (
        lax.all_to_all(queries, "head", split_axis=1, concat_axis=0, tiled=True),
        lax.all_to_all(keys, "head", split_axis=1, concat_axis=0, tiled=True),
        lax.all_to_all(values, "head", split_axis=1, concat_axis=0, tiled=True),
    )
    row_count = query_block.shape[0]
    query_heads = query_block.reshape(row_count, heads_dev, HEAD_DIM)
    key_heads = key_block.reshape(row_count, heads_dev, HEAD_DIM)
    value_heads = value_block.reshape(row_count, heads_dev, HEAD_DIM)
    kv_state = jnp.einsum(
        "thd,the->hde", key_heads, value_heads, preferred_element_type=jnp.float32
    )
    prefix = carried_in(kv_state, "seq", add_states, jnp.zeros_like(kv_state))
    carried = jnp.einsum(
        "thd,hde->the", query_heads, prefix.astype(jnp.bfloat16), preferred_element_type=jnp.float32
    )
    block_rows = min(512, row_count)
    parts_list = []
    for first_row in range(0, row_count, block_rows):
        last_row = min(first_row + block_rows, row_count)
        scores = jnp.einsum(
            "thd,shd->hts",
            query_heads[first_row:last_row],
            key_heads[:last_row],
            preferred_element_type=jnp.float32,
        )
        row_index = first_row + lax.broadcasted_iota(jnp.int32, (last_row - first_row, last_row), 0)
        col_index = lax.broadcasted_iota(jnp.int32, (last_row - first_row, last_row), 1)
        scores = jnp.where((col_index <= row_index)[None], scores, jnp.zeros_like(scores)).astype(
            jnp.bfloat16
        )
        parts_list.append(
            jnp.einsum(
                "hts,she->the", scores, value_heads[:last_row], preferred_element_type=jnp.float32
            )
        )
    within_block = jnp.concatenate(parts_list, axis=0)
    attended = carried + within_block
    mean_square = jnp.mean(attended * attended, axis=2, keepdims=True)
    gain_heads = norm_gain.reshape(heads_dev, HEAD_DIM)
    normed = (attended * lax.rsqrt(mean_square + 1e-06) * gain_heads[None]).astype(jnp.bfloat16)
    normed = normed.reshape(row_count, heads_dev * HEAD_DIM)
    returned = lax.all_to_all(normed, "head", split_axis=0, concat_axis=1, tiled=True)
    gathered = lax.all_gather(returned, "head", axis=0, tiled=True)
    outcome = jnp.dot(
        gathered,
        lax.all_gather(out_weight, "seq", axis=0, tiled=True),
        preferred_element_type=jnp.float32,
    )
    return outcome.astype(jnp.bfloat16)


def solution(mesh):
    return jax.shard_map(
        local,
        mesh=mesh,
        in_specs=(
            P(("seq", "head"), None),
            P(("seq", "head"), None),
            P(("seq", "head"), None),
            P("seq", "head"),
            P("head"),
        ),
        out_specs=P("seq", "head"),
        check_vma=False,
    )
```

profile of v0, /device:TPU:0, one launch (start us, length us, event | category | flops | bytes accessed | tf_op | source)
XLA Modules:
  0.0 361.1 jit_solution(12308427636008386715)
XLA Ops:
  6.5 2.4 copy.44
  8.9 4.2 %all-to-all-start.1 = ((bf16[128,2,2048]{2,0,1:T(8,128)(2,1)}), bf16[128,2,2048]{2,0,1:T(8,128)(2,1)S(1)}, u32[]{:S(2)}, u32[]{:S(2)}) async-start(bf16[128,2,2048]{2,0,1:T(8,128)(2,1)} %bitcast.38), calls=%async_computation.1 | async-start | bytes 2097152 | tf_op jit(solution)/shard_map/all_to_all | solution.py:29
  13.1 1.3 copy.17
  14.4 13.1 %all-to-all-done.1 = bf16[128,2,2048]{2,0,1:T(8,128)(2,1)S(1)} async-done(((bf16[128,2,2048]{2,0,1:T(8,128)(2,1)}), bf16[128,2,2048]{2,0,1:T(8,128)(2,1)S(1)}, u32[]{:S(2)}, u32[]{:S(2)}) %all-to-all-start.1) | async-done | bytes 1048608 | tf_op jit(solution)/shard_map/all_to_all | solution.py:29
  27.6 3.6 all-to-all-start
  31.2 0.0 all-gather.9.cloned.1.call-start
  31.2 0.2 copy.32
  31.4 0.8 copy.26
  32.2 12.2 %all-to-all-done = bf16[128,2,2048]{0,2,1:T(8,128)(2,1)S(1)} async-done(((bf16[128,2,2048]{0,2,1:T(8,128)(2,1)}), bf16[128,2,2048]{0,2,1:T(8,128)(2,1)S(1)}, u32[]{:S(2)}, u32[]{:S(2)}) %all-to-all-start) | async-done | bytes 1048608 | tf_op jit(solution)/shard_map/all_to_all | solution.py:28
  44.5 8.6 %copy.18 = bf16[2,128,2048]{1,0,2:T(2,128)(2,1)S(1)} copy(bf16[2,128,2048]{1,2,0:T(8,128)(2,1)S(1)} %bitcast.44) | data formatting | bytes 2097152 | tf_op jit(solution)/shard_map/all_to_all | solution.py:28
  53.1 0.7 reshape.42
  53.8 1.4 fusion.6
  55.3 0.0 all-gather.7.cloned.1.call-start
  55.3 0.7 all-gather.7.cloned.1.call-update
  56.1 1.0 copy.43
  57.1 3.6 all-to-all-start.2
  60.7 0.0 all-gather.5.cloned.1.call-start
  60.8 12.3 %all-to-all-done.2 = bf16[128,2,2048]{2,0,1:T(8,128)(2,1)S(1)} async-done(((bf16[128,2,2048]{2,0,1:T(8,128)(2,1)}), bf16[128,2,2048]{2,0,1:T(8,128)(2,1)S(1)}, u32[]{:S(2)}, u32[]{:S(2)}) %all-to-all-start.2) | async-done | bytes 1048608 | tf_op jit(solution)/shard_map/all_to_all | solution.py:27
  73.1 1.2 copy.33
  74.3 3.8 %fusion = f32[16,256,128]{1,2,0:T(8,128)} fusion(bf16[256,16,128]{0,2,1:T(8,128)(2,1)S(1)} %copy.26, bf16[256,16,128]{0,2,1:T(8,128)(2,1)S(1)} %reshape.42, pred[256,256]{1,0:T(8,128)(4,1)S(1)} %iota_compare_fusion, bf16[256,16,128]{2,1,0:T(8,128)(2,1)} %bitcast.47), kind=kOutput, calls=%fused_computation.6 | convolution fusion | flops 538968064 | bytes 5308416 | tf_op jit(solution)/shard_map/hts,she->the/dot_general | solution.py:58
  78.1 104.5 %all-gather.9.cloned.1.call-done = f32[256,128,128]{2,1,0:T(8,128)} async-done(((f32[16,128,128]{2,1,0:T(8,128)}), f32[256,128,128]{2,1,0:T(8,128)}) %all-gather.9.cloned.1.call-update) | async-done | bytes 16777232 | tf_op jit(solution)/shard_map/all_gather | solution.py:11
  182.6 0.1 broadcast_in_dim.16
  182.7 1.2 copy-done
  183.9 2.2 multiply_reduce_fusion
  186.2 0.3 multiply_convert_fusion
  186.5 0.3 all_to_all.59
  186.8 0.1 copy.27
  186.9 17.9 %all_to_all.67 = bf16[2,128,2048]{1,2,0:T(8,128)(2,1)} all-to-all(bf16[2,128,2048]{1,2,0:T(8,128)(2,1)S(1)} %copy.27), channel_id=1, replica_groups=mesh['seq'=16,'head'=2] {'head'}, dimensions={0} | all-to-all | bytes 2097152 | tf_op jit(solution)/shard_map/all_to_all | solution.py:68
  204.9 0.0 all-gather.5.cloned.1.call-update
  204.9 104.9 %all-gather.7.cloned.1.call-done = bf16[4096,2048]{1,0:T(8,128)(2,1)} async-done(((bf16[256,2048]{1,0:T(8,128)(2,1)}), bf16[4096,2048]{1,0:T(8,128)(2,1)}) %all-gather.7.cloned.1.call-update) | async-done | bytes 16777232 | tf_op jit(solution)/shard_map/all_gather | solution.py:72
  309.9 32.8 %all-gather.5.cloned.1.call-done = bf16[256,4096]{0,1:T(8,128)(2,1)} async-done(((bf16[128,4096]{0,1:T(8,128)(2,1)}), bf16[256,4096]{0,1:T(8,128)(2,1)}) %all-gather.5.cloned.1.call-update) | async-done | bytes 2097168 | tf_op jit(solution)/shard_map/all_gather | solution.py:69
  342.7 11.9 %convolution_convert_fusion = bf16[256,2048]{1,0:T(8,128)(2,1)} fusion(bf16[256,4096]{0,1:T(8,128)(2,1)} %all-gather.5.cloned.1.call-done, bf16[4096,2048]{1,0:T(8,128)(2,1)} %all-gather.7.cloned.1.call-done), kind=kOutput, calls=%fused_computation.2 | convolution fusion | flops 4295491584 | bytes 19922944 | tf_op jit(solution)/shard_map/dot_general | solution.py:70
  (11 shorter events, 0.1 us)
Async XLA Ops:
  6.5 6.6 %copy-start.1 = (bf16[128,4096]{1,0:T(8,128)(2,1)S(1)}, bf16[128,4096]{1,0:T(8,128)(2,1)}, u32[]{:S(2)}) copy-start(bf16[128,4096]{1,0:T(8,128)(2,1)} %param.8) | copy-start | bytes 3145732
  8.9 18.6 %all-to-all-start.1 = ((bf16[128,2,2048]{2,0,1:T(8,128)(2,1)}), bf16[128,2,2048]{2,0,1:T(8,128)(2,1)S(1)}, u32[]{:S(2)}, u32[]{:S(2)}) async-start(bf16[128,2,2048]{2,0,1:T(8,128)(2,1)} %bitcast.38), calls=%async_computation.1 | async-start | bytes 2097152 | tf_op jit(solution)/shard_map/all_to_all | solution.py:29
  27.6 16.9 %all-to-all-start = ((bf16[128,2,2048]{0,2,1:T(8,128)(2,1)}), bf16[128,2,2048]{0,2,1:T(8,128)(2,1)S(1)}, u32[]{:S(2)}, u32[]{:S(2)}) async-start(bf16[128,2,2048]{0,2,1:T(8,128)(2,1)} %bitcast.1), calls=%async_computation | async-start | bytes 2097152 | tf_op jit(solution)/shard_map/all_to_all | solution.py:28
  31.2 151.4 %all-gather.9.cloned.1.call-start = ((), (), s32[]{:S(2)}) async-start(), calls=%async_computation.6 | async-start | bytes 17825792 | tf_op jit(solution)/shard_map/all_gather | solution.py:11
  53.8 2.2 copy-start.2
  55.3 254.6 %all-gather.7.cloned.1.call-start = ((), (), s32[]{:S(2)}) async-start(), calls=%async_computation.5 | async-start | bytes 17825792 | tf_op jit(solution)/shard_map/all_gather | solution.py:72
  57.1 16.0 %all-to-all-start.2 = ((bf16[128,2,2048]{2,0,1:T(8,128)(2,1)}), bf16[128,2,2048]{2,0,1:T(8,128)(2,1)S(1)}, u32[]{:S(2)}, u32[]{:S(2)}) async-start(bf16[128,2,2048]{2,0,1:T(8,128)(2,1)} %bitcast.43), calls=%async_computation.2 | async-start | bytes 2097152 | tf_op jit(solution)/shard_map/all_to_all | solution.py:27
  60.7 282.0 %all-gather.5.cloned.1.call-start = ((), (), s32[]{:S(2)}) async-start(), calls=%async_computation.4 | async-start | bytes 3145728 | tf_op jit(solution)/shard_map/all_gather | solution.py:69
  182.7 1.2 copy-start
  183.9 2.2 copy-start.3
Sparse Core Ops, SparseCore 0:
  55.4 127.1 all-gather.8
  184.8 125.0 all-gather.6
  311.4 31.2 all-gather.4
where the time goes:
time: 362 us; the launch traced here: 361 us
  waiting for transfers between devices  281 us (78%)
  matrix products  19.3 us (5%)
  local copies, waits for them, and re-layouts  18 us (5%)
  blocking collectives  17.9 us (5%)
  between operations  13.3 us (4%)
  starting transfers between devices  11.5 us (3%)
    all_gather x1, waiting for transfers between devices, local(): lax.all_gather(out_weight, 'seq', axis=0, tiled=True)  105 us
    all_gather x1, waiting for transfers between devices, carried_in(): gathered = lax.all_gather(part, axis)  104 us
    all_gather x1, waiting for transfers between devices, local(): gathered = lax.all_gather(returned, 'head', axis=0, tiled=True)  32.8 us
    all_to_all x1, blocking collectives, local(): lax.all_to_all(normed, 'head', split_axis=0, concat_axis=1, tiled=True)  17.9 us
    all_to_all x1, waiting for transfers between devices, local(): lax.all_to_all(values, 'head', split_axis=1, concat_axis=0, tiled=True)  13.1 us
    all_to_all x1, waiting for transfers between devices, local(): lax.all_to_all(queries, 'head', split_axis=1, concat_axis=0, tiled=True)  12.3 us
    all_to_all x1, waiting for transfers between devices, local(): lax.all_to_all(keys, 'head', split_axis=1, concat_axis=0, tiled=True)  12.2 us
    dot_general x1, matrix products, local(): jnp.dot(gathered, lax.all_gather(out_weight, 'seq', axis=0, tiled=True),...  11.9 us
  transfers between devices with their start and end apart: 6, of which 6 were waited for; matrix products, arithmetic and copies ran while one was open for 3% of the time, Pallas kernels for 0%

commit v1 on v0

--- a/solution.py
+++ b/solution.py
@@ -4,6 +4,24 @@
 from jax.sharding import PartitionSpec as P
 
 HEAD_DIM = 128
+
+
+def ring_gather(value, axis, dim):
+    ways, here, step = (lax.axis_size(axis), lax.axis_index(axis), value.shape[dim])
+    shape = [n * ways if d == dim else n for d, n in enumerate(value.shape)]
+    full = lax.dynamic_update_slice_in_dim(
+        jnp.zeros(shape, value.dtype), value, here * step, axis=dim
+    )
+    going_up = going_down = value
+    for far in range(1, ways // 2 + 1):
+        going_up = lax.ppermute(going_up, axis, [(d, (d + 1) % ways) for d in range(ways)])
+        full = lax.dynamic_update_slice_in_dim(full, going_up, (here - far) % ways * step, axis=dim)
+        if 2 * far < ways:
+            going_down = lax.ppermute(going_down, axis, [(d, (d - 1) % ways) for d in range(ways)])
+            full = lax.dynamic_update_slice_in_dim(
+                full, going_down, (here + far) % ways * step, axis=dim
+            )
+    return full
 
 
 def carried_in(part, axis, combine, identity):
@@ -68,9 +86,7 @@
     returned = lax.all_to_all(normed, "head", split_axis=0, concat_axis=1, tiled=True)
     gathered = lax.all_gather(returned, "head", axis=0, tiled=True)
     outcome = jnp.dot(
-        gathered,
-        lax.all_gather(out_weight, "seq", axis=0, tiled=True),
-        preferred_element_type=jnp.float32,
+        gathered, ring_gather(out_weight, "seq", 0), preferred_element_type=jnp.float32
     )
     return outcome.astype(jnp.bfloat16)
 

time: 362 us -> 351 us (0.970)
  waiting for transfers between devices: 281 us -> 145 us
  starting transfers between devices: 11.5 us -> 110 us
  local copies, waits for them, and re-layouts: 18 us -> 59.6 us
  blocking collectives: 17.9 us -> 0 us
    all_gather x1 -> x0, waiting for transfers between devices: 105 us -> none  [local(): lax.all_gather(out_weight, 'seq', axis=0, tiled=True)]
    ppermute x0 -> x15, starting transfers between devices: none -> 95.3 us  [the longest x8 55.4 us: ring_gather(): lax.ppermute(going_up, axis, [(d, (d + 1) % ways) for d in range(ways)])]
    ppermute x0 -> x15, waiting for transfers between devices: none -> 91.9 us  [the longest x8 80.6 us: ring_gather(): lax.ppermute(going_up, axis, [(d, (d + 1) % ways) for d in range(ways)])]
    all_gather x1, waiting for transfers between devices: 104 us -> 17.3 us  [carried_in(): gathered = lax.all_gather(part, axis)]
    dynamic_update_slice x0 -> x16, local copies, waits for them, and re-layouts: none -> 32.5 us  [the longest x8 16.3 us: ring_gather(): lax.dynamic_update_slice_in_dim(full, going_up, (here - far) % ways * ste...]
    all_gather x1, waiting for transfers between devices: 32.8 us -> 4.32 us  [local(): gathered = lax.all_gather(returned, 'head', axis=0, tiled=True)]
    all_to_all x1 -> x0, blocking collectives: 17.9 us -> none  [local(): lax.all_to_all(normed, 'head', split_axis=0, concat_axis=1, tiled=True)]
    all_to_all x1, waiting for transfers between devices: 12.3 us -> 1.85 us  [local(): lax.all_to_all(queries, 'head', split_axis=1, concat_axis=0, tiled=True)]
  transfers between devices with their start and end apart: 6 -> 21, of which waited for: 6 -> 14; matrix products, arithmetic and copies ran while one was open for 3% -> 15% of each run, Pallas kernels for 0% -> 0%
where the time goes in v1:
time: 351 us; the launch traced here: 349 us
  waiting for transfers between devices  145 us (41%)
  starting transfers between devices  110 us (31%)
  local copies, waits for them, and re-layouts  59.6 us (17%)
  matrix products  19.7 us (6%)
  between operations  13.9 us (4%)
    ppermute x8, waiting for transfers between devices, ring_gather(): lax.ppermute(going_up, axis, [(d, (d + 1) % ways) for d in range(ways)])  80.6 us
    ppermute x8, starting transfers between devices, ring_gather(): lax.ppermute(going_up, axis, [(d, (d + 1) % ways) for d in range(ways)])  55.4 us
    ppermute x7, starting transfers between devices, ring_gather(): lax.ppermute(going_down, axis, [(d, (d - 1) % ways) for d in range(ways)])  40 us
    all_gather x1, waiting for transfers between devices, carried_in(): gathered = lax.all_gather(part, axis)  17.3 us
    dynamic_update_slice x8, local copies, waits for them, and re-layouts, ring_gather(): lax.dynamic_update_slice_in_dim(full, going_up, (here - far) % ways * ste...  16.3 us
    dynamic_update_slice x7, local copies, waits for them, and re-layouts, ring_gather(): lax.dynamic_update_slice_in_dim(full, going_down, (here + far) % ways * s...  15.1 us
    all_to_all x1, waiting for transfers between devices, local(): lax.all_to_all(keys, 'head', split_axis=1, concat_axis=0, tiled=True)  12.2 us
    all_to_all x1, waiting for transfers between devices, local(): lax.all_to_all(values, 'head', split_axis=1, concat_axis=0, tiled=True)  12.2 us
  transfers between devices with their start and end apart: 21, of which 14 were waited for; matrix products, arithmetic and copies ran while one was open for 15% of the time, Pallas kernels for 0%

profile of v1, /device:TPU:0, one launch (start us, length us, event | category | flops | bytes accessed | tf_op | source)
XLA Modules:
  0.0 349.2 jit_solution(17798399090590680699)
XLA Ops:
  8.8 4.2 %all-to-all-start.1 = ((bf16[128,2,2048]{2,0,1:T(8,128)(2,1)}), bf16[128,2,2048]{2,0,1:T(8,128)(2,1)S(1)}, u32[]{:S(2)}, u32[]{:S(2)}) async-start(bf16[128,2,2048]{2,0,1:T(8,128)(2,1)} %bitcast.38), calls=%async_computation.1 | async-start | bytes 2097152 | tf_op jit(solution)/shard_map/all_to_all | solution.py:47
  15.3 12.2 %all-to-all-done.1 = bf16[128,2,2048]{2,0,1:T(8,128)(2,1)S(1)} async-done(((bf16[128,2,2048]{2,0,1:T(8,128)(2,1)}), bf16[128,2,2048]{2,0,1:T(8,128)(2,1)S(1)}, u32[]{:S(2)}, u32[]{:S(2)}) %all-to-all-start.1) | async-done | bytes 1048608 | tf_op jit(solution)/shard_map/all_to_all | solution.py:47
  27.5 3.6 %all-to-all-start = ((bf16[128,2,2048]{0,2,1:T(8,128)(2,1)}), bf16[128,2,2048]{0,2,1:T(8,128)(2,1)S(1)}, u32[]{:S(2)}, u32[]{:S(2)}) async-start(bf16[128,2,2048]{0,2,1:T(8,128)(2,1)} %bitcast.1), calls=%async_computation | async-start | bytes 2097152 | tf_op jit(solution)/shard_map/all_to_all | solution.py:46
  32.1 12.2 %all-to-all-done = bf16[128,2,2048]{0,2,1:T(8,128)(2,1)S(1)} async-done(((bf16[128,2,2048]{0,2,1:T(8,128)(2,1)}), bf16[128,2,2048]{0,2,1:T(8,128)(2,1)S(1)}, u32[]{:S(2)}, u32[]{:S(2)}) %all-to-all-start) | async-done | bytes 1048608 | tf_op jit(solution)/shard_map/all_to_all | solution.py:46
  44.4 8.6 %copy.18 = bf16[2,128,2048]{1,0,2:T(2,128)(2,1)S(1)} copy(bf16[2,128,2048]{1,2,0:T(8,128)(2,1)S(1)} %bitcast.45) | data formatting | bytes 2097152 | tf_op jit(solution)/shard_map/all_to_all | solution.py:46
  55.3 4.4 %collective-permute-start.1 = (bf16[256,2048]{1,0:T(8,128)(2,1)}, bf16[256,2048]{1,0:T(8,128)(2,1)S(1)}, u32[]{:S(2)}, u32[]{:S(2)}) collective-permute-start(bf16[256,2048]{1,0:T(8,128)(2,1)} %param.10), channel_id=1, source_target_pairs={{0,30},{2,0},{4,2},{6,4},{8,6},{10,8},{12,10},{14,12},{16,14},{18,... | collective-permute-start | bytes 3145736 | tf_op jit(solution)/shard_map/ppermute | solution.py:20
  59.7 17.5 %collective-permute-done = bf16[256,2048]{1,0:T(8,128)(2,1)S(1)} collective-permute-done((bf16[256,2048]{1,0:T(8,128)(2,1)}, bf16[256,2048]{1,0:T(8,128)(2,1)S(1)}, u32[]{:S(2)}, u32[]{:S(2)}) %collective-permute-start) | collective-permute-done | bytes 1048608 | tf_op jit(solution)/shard_map/ppermute | solution.py:17
  77.2 14.0 %collective-permute-start.2 = (bf16[256,2048]{1,0:T(8,128)(2,1)S(1)}, bf16[256,2048]{1,0:T(8,128)(2,1)S(1)}, u32[]{:S(2)}, u32[]{:S(2)}) collective-permute-start(bf16[256,2048]{1,0:T(8,128)(2,1)S(1)} %collective-permute-done), channel_id=1, source_target_pairs={{0,2},{2,4},{4,6},{6,8},{8,10},{10,12},{12,14},{14,16},{16,18},{18... | collective-permute-start | bytes 3145736 | tf_op jit(solution)/shard_map/ppermute | solution.py:17
  91.3 25.3 %collective-permute-done.2 = bf16[256,2048]{1,0:T(8,128)(2,1)S(1)} collective-permute-done((bf16[256,2048]{1,0:T(8,128)(2,1)S(1)}, bf16[256,2048]{1,0:T(8,128)(2,1)S(1)}, u32[]{:S(2)}, u32[]{:S(2)}) %collective-permute-start.2) | collective-permute-done | bytes 1048608 | tf_op jit(solution)/shard_map/ppermute | solution.py:17
  117.7 4.7 %collective-permute-start.5 = (bf16[256,2048]{1,0:T(8,128)(2,1)S(1)}, bf16[256,2048]{1,0:T(8,128)(2,1)}, u32[]{:S(2)}, u32[]{:S(2)}) collective-permute-start(bf16[256,2048]{1,0:T(8,128)(2,1)S(1)} %collective-permute-done.3), channel_id=1, source_target_pairs={{0,30},{2,0},{4,2},{6,4},{8,6},{10,8},{12,10},{14,12},{16,14},{18,... | collective-permute-start | bytes 3145736 | tf_op jit(solution)/shard_map/ppermute | solution.py:20
  122.4 26.1 %collective-permute-done.4 = bf16[256,2048]{1,0:T(8,128)(2,1)} collective-permute-done((bf16[256,2048]{1,0:T(8,128)(2,1)S(1)}, bf16[256,2048]{1,0:T(8,128)(2,1)}, u32[]{:S(2)}, u32[]{:S(2)}) %collective-permute-start.4) | collective-permute-done | bytes 1048608 | tf_op jit(solution)/shard_map/ppermute | solution.py:17
  149.1 8.1 %collective-permute-done.5 = bf16[256,2048]{1,0:T(8,128)(2,1)} collective-permute-done((bf16[256,2048]{1,0:T(8,128)(2,1)S(1)}, bf16[256,2048]{1,0:T(8,128)(2,1)}, u32[]{:S(2)}, u32[]{:S(2)}) %collective-permute-start.5) | collective-permute-done | bytes 1048608 | tf_op jit(solution)/shard_map/ppermute | solution.py:20
  157.1 4.7 %collective-permute-start.7 = (bf16[256,2048]{1,0:T(8,128)(2,1)}, bf16[256,2048]{1,0:T(8,128)(2,1)}, u32[]{:S(2)}, u32[]{:S(2)}) collective-permute-start(bf16[256,2048]{1,0:T(8,128)(2,1)} %collective-permute-done.5), channel_id=1, source_target_pairs={{0,30},{2,0},{4,2},{6,4},{8,6},{10,8},{12,10},{14,12},{16,14},{18,... | collective-permute-start | bytes 3145736 | tf_op jit(solution)/shard_map/ppermute | solution.py:20
  164.2 3.6 %all-to-all-start.2 = ((bf16[128,2,2048]{2,0,1:T(8,128)(2,1)}), bf16[128,2,2048]{2,0,1:T(8,128)(2,1)S(1)}, u32[]{:S(2)}, u32[]{:S(2)}) async-start(bf16[128,2,2048]{2,0,1:T(8,128)(2,1)} %bitcast.42), calls=%async_computation.2 | async-start | bytes 2097152 | tf_op jit(solution)/shard_map/all_to_all | solution.py:45
  168.1 6.1 %broadcast_in_dim.22 = bf16[4096,2048]{1,0:T(8,128)(2,1)} broadcast(bf16[]{:T(256)} %constant.110.clone.1), dimensions={} | broadcast | bytes 16777218 | tf_op jit(solution)/shard_map/broadcast_in_dim | solution.py:13
  178.3 6.1 %collective-permute-done.6 = bf16[256,2048]{1,0:T(8,128)(2,1)} collective-permute-done((bf16[256,2048]{1,0:T(8,128)(2,1)}, bf16[256,2048]{1,0:T(8,128)(2,1)}, u32[]{:S(2)}, u32[]{:S(2)}) %collective-permute-start.6) | collective-permute-done | bytes 1048608 | tf_op jit(solution)/shard_map/ppermute | solution.py:17
  184.4 17.6 %collective-permute-start.8 = (bf16[256,2048]{1,0:T(8,128)(2,1)}, bf16[256,2048]{1,0:T(8,128)(2,1)}, u32[]{:S(2)}, u32[]{:S(2)}) collective-permute-start(bf16[256,2048]{1,0:T(8,128)(2,1)} %collective-permute-done.6), channel_id=1, source_target_pairs={{0,2},{2,4},{4,6},{6,8},{8,10},{10,12},{12,14},{14,16},{16,18},{18... | collective-permute-start | bytes 3145736 | tf_op jit(solution)/shard_map/ppermute | solution.py:17
  202.1 3.9 %fusion = f32[16,256,128]{1,2,0:T(8,128)} fusion(bf16[256,16,128]{0,2,1:T(8,128)(2,1)S(1)} %copy.26, bf16[256,16,128]{0,2,1:T(8,128)(2,1)S(1)} %reshape.42, pred[256,256]{1,0:T(8,128)(4,1)S(1)} %iota_compare_fusion, bf16[256,16,128]{2,1,0:T(8,128)(2,1)} %bitcast.47), kind=kOutput, calls=%fused_computation.6 | convolution fusion | flops 538968064 | bytes 5308416 | tf_op jit(solution)/shard_map/hts,she->the/dot_general | solution.py:76
  206.0 2.4 constant_dynamic-update-slice_fusion.14
  213.0 21.3 %collective-permute-start.10 = (bf16[256,2048]{1,0:T(8,128)(2,1)}, bf16[256,2048]{1,0:T(8,128)(2,1)}, u32[]{:S(2)}, u32[]{:S(2)}) collective-permute-start(bf16[256,2048]{1,0:T(8,128)(2,1)} %collective-permute-done.8), channel_id=1, source_target_pairs={{0,2},{2,4},{4,6},{6,8},{8,10},{10,12},{12,14},{14,16},{16,18},{18... | collective-permute-start | bytes 3145736 | tf_op jit(solution)/shard_map/ppermute | solution.py:17
  234.3 17.3 %all-gather.6.cloned.1.call-done = f32[256,128,128]{2,1,0:T(8,128)} async-done(((f32[16,128,128]{2,1,0:T(8,128)}), f32[256,128,128]{2,1,0:T(8,128)}) %all-gather.6.cloned.1.call-update) | async-done | bytes 16777232 | tf_op jit(solution)/shard_map/all_gather | solution.py:29
  251.8 2.5 multiply_reduce_fusion
  256.1 3.6 %all-to-all-start.3 = ((bf16[2,128,2048]{1,2,0:T(8,128)(2,1)}), bf16[2,128,2048]{1,2,0:T(8,128)(2,1)S(1)}, u32[]{:S(2)}, u32[]{:S(2)}) async-start(bf16[2,128,2048]{1,2,0:T(8,128)(2,1)} %copy.27), calls=%async_computation.3 | async-start | bytes 2097152 | tf_op jit(solution)/shard_map/all_to_all | solution.py:86
  259.7 2.3 constant_dynamic-update-slice_fusion.11
  268.4 5.5 %all-to-all-done.3 = bf16[2,128,2048]{1,2,0:T(8,128)(2,1)S(1)} async-done(((bf16[2,128,2048]{1,2,0:T(8,128)(2,1)}), bf16[2,128,2048]{1,2,0:T(8,128)(2,1)S(1)}, u32[]{:S(2)}, u32[]{:S(2)}) %all-to-all-start.3) | async-done | bytes 1048608 | tf_op jit(solution)/shard_map/all_to_all | solution.py:86
  277.2 2.4 constant_dynamic-update-slice_fusion.7
  279.6 26.1 %collective-permute-start.13 = (bf16[256,2048]{1,0:T(8,128)(2,1)}, bf16[256,2048]{1,0:T(8,128)(2,1)S(1)}, u32[]{:S(2)}, u32[]{:S(2)}) collective-permute-start(bf16[256,2048]{1,0:T(8,128)(2,1)} %collective-permute-done.11), channel_id=1, source_target_pairs={{0,30},{2,0},{4,2},{6,4},{8,6},{10,8},{12,10},{14,12},{16,14},{18,... | collective-permute-start | bytes 3145736 | tf_op jit(solution)/shard_map/ppermute | solution.py:20
  305.7 2.4 constant_dynamic-update-slice_fusion.6
  308.1 2.3 constant_dynamic-update-slice_fusion.5
  319.5 5.5 %collective-permute-done.14 = bf16[256,2048]{1,0:T(8,128)(2,1)S(1)} collective-permute-done((bf16[256,2048]{1,0:T(8,128)(2,1)S(1)}, bf16[256,2048]{1,0:T(8,128)(2,1)S(1)}, u32[]{:S(2)}, u32[]{:S(2)}) %collective-permute-start.14) | collective-permute-done | bytes 1048608 | tf_op jit(solution)/shard_map/ppermute | solution.py:17
  326.2 4.3 %all-gather.4.cloned.1.call-done = bf16[256,4096]{0,1:T(8,128)(2,1)} async-done(((bf16[128,4096]{0,1:T(8,128)(2,1)}), bf16[256,4096]{0,1:T(8,128)(2,1)}) %all-gather.4.cloned.1.call-update) | async-done | bytes 2097168 | tf_op jit(solution)/shard_map/all_gather | solution.py:87
  330.5 11.9 %convolution_convert_fusion = bf16[256,2048]{1,0:T(8,128)(2,1)} fusion(bf16[256,4096]{0,1:T(8,128)(2,1)} %all-gather.4.cloned.1.call-done, bf16[4096,2048]{1,0:T(8,128)(2,1)} %constant_dynamic-update-slice_fusion), kind=kOutput, calls=%fused_computation.2 | convolution fusion | flops 4295491584 | bytes 19922944 | tf_op jit(solution)/shard_map/dot_general | solution.py:88
  (62 shorter events, 42.4 us)
Async XLA Ops:
  8.8 18.6 %all-to-all-start.1 = ((bf16[128,2,2048]{2,0,1:T(8,128)(2,1)}), bf16[128,2,2048]{2,0,1:T(8,128)(2,1)S(1)}, u32[]{:S(2)}, u32[]{:S(2)}) async-start(bf16[128,2,2048]{2,0,1:T(8,128)(2,1)} %bitcast.38), calls=%async_computation.1 | async-start | bytes 2097152 | tf_op jit(solution)/shard_map/all_to_all | solution.py:47
  27.5 16.9 %all-to-all-start = ((bf16[128,2,2048]{0,2,1:T(8,128)(2,1)}), bf16[128,2,2048]{0,2,1:T(8,128)(2,1)S(1)}, u32[]{:S(2)}, u32[]{:S(2)}) async-start(bf16[128,2,2048]{0,2,1:T(8,128)(2,1)} %bitcast.1), calls=%async_computation | async-start | bytes 2097152 | tf_op jit(solution)/shard_map/all_to_all | solution.py:46
  31.1 220.6 %all-gather.6.cloned.1.call-start = ((), (), s32[]{:S(2)}) async-start(), calls=%async_computation.5 | async-start | bytes 17825792 | tf_op jit(solution)/shard_map/all_gather | solution.py:29
  55.2 22.0 %collective-permute-start = (bf16[256,2048]{1,0:T(8,128)(2,1)}, bf16[256,2048]{1,0:T(8,128)(2,1)S(1)}, u32[]{:S(2)}, u32[]{:S(2)}) collective-permute-start(bf16[256,2048]{1,0:T(8,128)(2,1)} %param.10), channel_id=1, source_target_pairs={{0,2},{2,4},{4,6},{6,8},{8,10},{10,12},{12,14},{14,16},{16,18},{18... | collective-permute-start | bytes 3145736 | tf_op jit(solution)/shard_map/ppermute | solution.py:17
  55.3 36.0 %collective-permute-start.1 = (bf16[256,2048]{1,0:T(8,128)(2,1)}, bf16[256,2048]{1,0:T(8,128)(2,1)S(1)}, u32[]{:S(2)}, u32[]{:S(2)}) collective-permute-start(bf16[256,2048]{1,0:T(8,128)(2,1)} %param.10), channel_id=1, source_target_pairs={{0,30},{2,0},{4,2},{6,4},{8,6},{10,8},{12,10},{14,12},{16,14},{18,... | collective-permute-start | bytes 3145736 | tf_op jit(solution)/shard_map/ppermute | solution.py:20
  77.2 79.9 %copy-start.3 = (bf16[256,2048]{1,0:T(8,128)(2,1)}, bf16[256,2048]{1,0:T(8,128)(2,1)S(1)}, u32[]{:S(2)}) copy-start(bf16[256,2048]{1,0:T(8,128)(2,1)S(1)} %collective-permute-done) | copy-start | bytes 3145732
  77.2 39.4 %collective-permute-start.2 = (bf16[256,2048]{1,0:T(8,128)(2,1)S(1)}, bf16[256,2048]{1,0:T(8,128)(2,1)S(1)}, u32[]{:S(2)}, u32[]{:S(2)}) collective-permute-start(bf16[256,2048]{1,0:T(8,128)(2,1)S(1)} %collective-permute-done), channel_id=1, source_target_pairs={{0,2},{2,4},{4,6},{6,8},{8,10},{10,12},{12,14},{14,16},{16,18},{18... | collective-permute-start | bytes 3145736 | tf_op jit(solution)/shard_map/ppermute | solution.py:17
  91.3 70.6 %copy-start.4 = (bf16[256,2048]{1,0:T(8,128)(2,1)}, bf16[256,2048]{1,0:T(8,128)(2,1)S(1)}, u32[]{:S(2)}) copy-start(bf16[256,2048]{1,0:T(8,128)(2,1)S(1)} %collective-permute-done.1) | copy-start | bytes 3145732
  91.3 26.4 %collective-permute-start.3 = (bf16[256,2048]{1,0:T(8,128)(2,1)S(1)}, bf16[256,2048]{1,0:T(8,128)(2,1)S(1)}, u32[]{:S(2)}, u32[]{:S(2)}) collective-permute-start(bf16[256,2048]{1,0:T(8,128)(2,1)S(1)} %collective-permute-done.1), channel_id=1, source_target_pairs={{0,30},{2,0},{4,2},{6,4},{8,6},{10,8},{12,10},{14,12},{16,14},{18,... | collective-permute-start | bytes 3145736 | tf_op jit(solution)/shard_map/ppermute | solution.py:20
  116.6 45.3 %copy-start.5 = (bf16[256,2048]{1,0:T(8,128)(2,1)}, bf16[256,2048]{1,0:T(8,128)(2,1)S(1)}, u32[]{:S(2)}) copy-start(bf16[256,2048]{1,0:T(8,128)(2,1)S(1)} %collective-permute-done.2) | copy-start | bytes 3145732
  116.6 31.9 %collective-permute-start.4 = (bf16[256,2048]{1,0:T(8,128)(2,1)S(1)}, bf16[256,2048]{1,0:T(8,128)(2,1)}, u32[]{:S(2)}, u32[]{:S(2)}) collective-permute-start(bf16[256,2048]{1,0:T(8,128)(2,1)S(1)} %collective-permute-done.2), channel_id=1, source_target_pairs={{0,2},{2,4},{4,6},{6,8},{8,10},{10,12},{12,14},{14,16},{16,18},{18... | collective-permute-start | bytes 3145736 | tf_op jit(solution)/shard_map/ppermute | solution.py:17
  117.7 46.5 %copy-start.2 = (bf16[256,2048]{1,0:T(8,128)(2,1)}, bf16[256,2048]{1,0:T(8,128)(2,1)S(1)}, u32[]{:S(2)}) copy-start(bf16[256,2048]{1,0:T(8,128)(2,1)S(1)} %collective-permute-done.3) | copy-start | bytes 3145732
  117.7 39.5 %collective-permute-start.5 = (bf16[256,2048]{1,0:T(8,128)(2,1)S(1)}, bf16[256,2048]{1,0:T(8,128)(2,1)}, u32[]{:S(2)}, u32[]{:S(2)}) collective-permute-start(bf16[256,2048]{1,0:T(8,128)(2,1)S(1)} %collective-permute-done.3), channel_id=1, source_target_pairs={{0,30},{2,0},{4,2},{6,4},{8,6},{10,8},{12,10},{14,12},{16,14},{18,... | collective-permute-start | bytes 3145736 | tf_op jit(solution)/shard_map/ppermute | solution.py:20
  148.5 35.9 %collective-permute-start.6 = (bf16[256,2048]{1,0:T(8,128)(2,1)}, bf16[256,2048]{1,0:T(8,128)(2,1)}, u32[]{:S(2)}, u32[]{:S(2)}) collective-permute-start(bf16[256,2048]{1,0:T(8,128)(2,1)} %collective-permute-done.4), channel_id=1, source_target_pairs={{0,2},{2,4},{4,6},{6,8},{8,10},{10,12},{12,14},{14,16},{16,18},{18... | collective-permute-start | bytes 3145736 | tf_op jit(solution)/shard_map/ppermute | solution.py:17
  157.1 44.9 %collective-permute-start.7 = (bf16[256,2048]{1,0:T(8,128)(2,1)}, bf16[256,2048]{1,0:T(8,128)(2,1)}, u32[]{:S(2)}, u32[]{:S(2)}) collective-permute-start(bf16[256,2048]{1,0:T(8,128)(2,1)} %collective-permute-done.5), channel_id=1, source_target_pairs={{0,30},{2,0},{4,2},{6,4},{8,6},{10,8},{12,10},{14,12},{16,14},{18,... | collective-permute-start | bytes 3145736 | tf_op jit(solution)/shard_map/ppermute | solution.py:20
  164.2 13.0 %all-to-all-start.2 = ((bf16[128,2,2048]{2,0,1:T(8,128)(2,1)}), bf16[128,2,2048]{2,0,1:T(8,128)(2,1)S(1)}, u32[]{:S(2)}, u32[]{:S(2)}) async-start(bf16[128,2,2048]{2,0,1:T(8,128)(2,1)} %bitcast.42), calls=%async_computation.2 | async-start | bytes 2097152 | tf_op jit(solution)/shard_map/all_to_all | solution.py:45
  168.1 6.2 %copy-start.1 = (bf16[256,2048]{1,0:T(8,128)(2,1)S(1)}, bf16[256,2048]{1,0:T(8,128)(2,1)}, u32[]{:S(2)}) copy-start(bf16[256,2048]{1,0:T(8,128)(2,1)} %param.10) | copy-start | bytes 3145732
  184.4 28.6 %collective-permute-start.8 = (bf16[256,2048]{1,0:T(8,128)(2,1)}, bf16[256,2048]{1,0:T(8,128)(2,1)}, u32[]{:S(2)}, u32[]{:S(2)}) collective-permute-start(bf16[256,2048]{1,0:T(8,128)(2,1)} %collective-permute-done.6), channel_id=1, source_target_pairs={{0,2},{2,4},{4,6},{6,8},{8,10},{10,12},{12,14},{14,16},{16,18},{18... | collective-permute-start | bytes 3145736 | tf_op jit(solution)/shard_map/ppermute | solution.py:17
  202.1 32.3 %collective-permute-start.9 = (bf16[256,2048]{1,0:T(8,128)(2,1)}, bf16[256,2048]{1,0:T(8,128)(2,1)}, u32[]{:S(2)}, u32[]{:S(2)}) collective-permute-start(bf16[256,2048]{1,0:T(8,128)(2,1)} %collective-permute-done.7), channel_id=1, source_target_pairs={{0,30},{2,0},{4,2},{6,4},{8,6},{10,8},{12,10},{14,12},{16,14},{18,... | collective-permute-start | bytes 3145736 | tf_op jit(solution)/shard_map/ppermute | solution.py:20
  202.1 52.2 %copy-start.6 = (f32[2048]{0:T(1024)S(1)}, f32[2048]{0:T(1024)}, u32[]{:S(2)}) copy-start(f32[2048]{0:T(1024)} %param.11) | copy-start | bytes 24580
  213.0 49.0 %collective-permute-start.10 = (bf16[256,2048]{1,0:T(8,128)(2,1)}, bf16[256,2048]{1,0:T(8,128)(2,1)}, u32[]{:S(2)}, u32[]{:S(2)}) collective-permute-start(bf16[256,2048]{1,0:T(8,128)(2,1)} %collective-permute-done.8), channel_id=1, source_target_pairs={{0,2},{2,4},{4,6},{6,8},{8,10},{10,12},{12,14},{14,16},{16,18},{18... | collective-permute-start | bytes 3145736 | tf_op jit(solution)/shard_map/ppermute | solution.py:17
  234.3 45.3 %collective-permute-start.11 = (bf16[256,2048]{1,0:T(8,128)(2,1)}, bf16[256,2048]{1,0:T(8,128)(2,1)}, u32[]{:S(2)}, u32[]{:S(2)}) collective-permute-start(bf16[256,2048]{1,0:T(8,128)(2,1)} %collective-permute-done.9), channel_id=1, source_target_pairs={{0,30},{2,0},{4,2},{6,4},{8,6},{10,8},{12,10},{14,12},{16,14},{18,... | collective-permute-start | bytes 3145736 | tf_op jit(solution)/shard_map/ppermute | solution.py:20
  256.1 17.8 %all-to-all-start.3 = ((bf16[2,128,2048]{1,2,0:T(8,128)(2,1)}), bf16[2,128,2048]{1,2,0:T(8,128)(2,1)S(1)}, u32[]{:S(2)}, u32[]{:S(2)}) async-start(bf16[2,128,2048]{1,2,0:T(8,128)(2,1)} %copy.27), calls=%async_computation.3 | async-start | bytes 2097152 | tf_op jit(solution)/shard_map/all_to_all | solution.py:86
  259.7 70.8 %all-gather.4.cloned.1.call-start = ((), (), s32[]{:S(2)}) async-start(), calls=%async_computation.4 | async-start | bytes 3145728 | tf_op jit(solution)/shard_map/all_gather | solution.py:87
  262.1 46.0 %collective-permute-start.12 = (bf16[256,2048]{1,0:T(8,128)(2,1)}, bf16[256,2048]{1,0:T(8,128)(2,1)S(1)}, u32[]{:S(2)}, u32[]{:S(2)}) collective-permute-start(bf16[256,2048]{1,0:T(8,128)(2,1)} %collective-permute-done.10), channel_id=1, source_target_pairs={{0,2},{2,4},{4,6},{6,8},{8,10},{10,12},{12,14},{14,16},{16,18},{18... | collective-permute-start | bytes 3145736 | tf_op jit(solution)/shard_map/ppermute | solution.py:17
  273.9 1.0 copy-start
  279.6 38.7 %collective-permute-start.13 = (bf16[256,2048]{1,0:T(8,128)(2,1)}, bf16[256,2048]{1,0:T(8,128)(2,1)S(1)}, u32[]{:S(2)}, u32[]{:S(2)}) collective-permute-start(bf16[256,2048]{1,0:T(8,128)(2,1)} %collective-permute-done.11), channel_id=1, source_target_pairs={{0,30},{2,0},{4,2},{6,4},{8,6},{10,8},{12,10},{14,12},{16,14},{18,... | collective-permute-start | bytes 3145736 | tf_op jit(solution)/shard_map/ppermute | solution.py:20
  308.1 16.9 %collective-permute-start.14 = (bf16[256,2048]{1,0:T(8,128)(2,1)S(1)}, bf16[256,2048]{1,0:T(8,128)(2,1)S(1)}, u32[]{:S(2)}, u32[]{:S(2)}) collective-permute-start(bf16[256,2048]{1,0:T(8,128)(2,1)S(1)} %collective-permute-done.12), channel_id=1, source_target_pairs={{0,2},{2,4},{4,6},{6,8},{8,10},{10,12},{12,14},{14,16},{16,18},{18... | collective-permute-start | bytes 3145736 | tf_op jit(solution)/shard_map/ppermute | solution.py:17
Sparse Core Ops, SparseCore 0:
  55.3 196.2 all-gather.5
  275.0 55.4 all-gather.3
